TPU v7x, 32 devices: a whole 2x2x4 slice. The times are simulated.
32 devices in a mesh: grp: 2 (over x), tile: 16 (over z, y, core).
Axes of the slice: x: 2, y: 2, z: 4, core: 2. Of those that a mesh axis runs over, the one named last changes fastest.
Arguments:
- latent: float32 [32, 1024, 128], P(None, ('grp', 'tile')), parts along dimension 1, may hold values from -6 to 6
- observed: float32 [32, 1024, 128], P(None, ('grp', 'tile')), parts along dimension 1, may hold values from -6 to 6
- noise: float32 [32, 1024, 128], P(None, ('grp', 'tile')), parts along dimension 1, may hold values from -6 to 6
- cloudy: int32 [128], P(('grp', 'tile')), parts along dimension 0, may hold values from 0 to 1, as said below
- timestep: int32 [2], P('grp'), parts along dimension 0, may hold values from 200 to 800
- pos_embed: bfloat16 [256, 2048], replicated, may hold values from -3 to 3
- embed_w: bfloat16 [128, 2048], replicated, may hold values from -0.5 to 0.5
- mod_w: bfloat16 [256, 6144], P(None, 'tile'), may hold values from -0.375 to 0.375
- wq: bfloat16 [2048, 1024], P('tile')
- wk: bfloat16 [2048, 1024], P('tile')
- wv: bfloat16 [2048, 1024], P('tile'), may hold values from -0.125 to 0.125
- wo: bfloat16 [1024, 2048], P(None, 'tile'), may hold values from -0.1875 to 0.1875
- q_gain: float32 [128], replicated, may hold values from 0.6 to 4.2
- k_gain: float32 [128], replicated, may hold values from 0.6 to 4.2
- out_w: bfloat16 [2048, 128], replicated, may hold values from -0.125 to 0.125
- conv_w: float32 [9, 32, 32], replicated, may hold values from -0.375 to 0.375
Outputs:
- estimate: float32 [32, 1024, 128], P(None, ('grp', 'tile')), parts along dimension 1
- next_latent: float32 [32, 1024, 128], P(None, ('grp', 'tile')), parts along dimension 1
There are 2 independent parts, one for each index of `grp`. A program takes and returns all parts, laid end to end along the dimension named above; an argument that names none is the same for every part. Nothing has to cross between parts.
Inputs may be any that keep to these rules, and one draw needn't show every extreme that they name: Exactly 16 tiles of a part are cloudy; each band of 4 tiles holds at most 3 of them, and some band holds exactly 3.
All inputs are finite; a program needn't handle non-finite values.
Results may differ from a plain program's by a relative error of at most 0.0033.
Values may be sent and summed in bfloat16 or wider, within the bound.
No kernel may reach another device: no remote copies, remote signals or barrier semaphores. Data moves between devices by JAX's collectives and lax.ppermute only.
A program may use at most 128 MiB of HBM per device.

v0:
```python
import math
import jax
import jax.numpy as jnp
from jax import lax
from jax.sharding import PartitionSpec as P

HD = 128
PATCH = 2
MAXOWN = 3
TSTEPS = 1000
STRIDE = 20


def padded_2(block, sides, width):
    for axis, dim in sides:
        count = lax.axis_size(axis)
        forward = [(i, i + 1) for i in range(count - 1)]
        backward = [(target, source) for source, target in forward]
        low = lax.ppermute(
            lax.slice_in_dim(block, block.shape[dim] - width, None, axis=dim), axis, forward
        )
        high = lax.ppermute(lax.slice_in_dim(block, 0, width, axis=dim), axis, backward)
        block = jnp.concatenate([low, block, high], axis=dim)
    return block


def plan(step):
    theta = (step / TSTEPS + 0.008) / 1.008 * (math.pi / 2)
    return (jnp.cos(theta), jnp.sin(theta))


def time_features(step, width):
    half = width // 2
    freqs = jnp.exp(-math.log(10000.0) * jnp.arange(half, dtype=jnp.float32) / half)
    angles = step * freqs
    code = jnp.concatenate([jnp.cos(angles), jnp.sin(angles)])[None, :]
    return jax.nn.silu(code).astype(jnp.bfloat16)


def layer_norm(values):
    center = values - jnp.mean(values, axis=-1, keepdims=True)
    spread = jnp.mean(center * center, axis=-1, keepdims=True)
    return center * lax.rsqrt(spread + 1e-06)


def head_norm(proj, gain, count, tokens_tile):
    shaped = proj.reshape(count, tokens_tile, -1, HD)
    scaled = shaped * lax.rsqrt(jnp.mean(shaped * shaped, axis=-1, keepdims=True) + 1e-06)
    return (scaled * gain).astype(jnp.bfloat16)


def band_tiles(band, tile_side):
    channels, band_rows, band_cols = band.shape
    tiles_here = band_cols // (tile_side * PATCH)
    shaped = band.reshape(channels, tile_side, PATCH, tiles_here, tile_side, PATCH)
    return jnp.transpose(shaped, (3, 1, 4, 2, 5, 0)).reshape(
        tiles_here, tile_side * tile_side, PATCH * PATCH * channels
    )


def band_pixels(tiled, tile_side, channels):
    tiles_here = tiled.shape[0]
    shaped = tiled.reshape(tiles_here, tile_side, tile_side, PATCH, PATCH, channels)
    return jnp.transpose(shaped, (5, 1, 3, 0, 2, 4)).reshape(
        channels, tile_side * PATCH, tiles_here * tile_side * PATCH
    )


def add_rows(left, shard_rows):
    return jnp.dot(left, shard_rows, preferred_element_type=jnp.float32)


def denoise(
    chosen,
    embed_w,
    pos_embed,
    shift_vec,
    scale_vec,
    gate_vec,
    wq,
    wk,
    wv,
    wo,
    q_gain,
    k_gain,
    out_w,
):
    count, tokens_tile, token_values = chosen.shape
    row_count = count * tokens_tile
    flat = chosen.reshape(row_count, token_values)
    hidden0 = jnp.dot(flat, embed_w, preferred_element_type=jnp.float32).reshape(
        count, tokens_tile, -1
    )
    hidden0 = (hidden0 + pos_embed.astype(jnp.float32)[None]).reshape(row_count, -1)
    modulated = (layer_norm(hidden0) * (1.0 + scale_vec) + shift_vec).astype(jnp.bfloat16)

    def add_one(shard_rows):
        return add_rows(modulated, shard_rows)

    query_all = add_one(lax.all_gather(wq, "tile", axis=0, tiled=True))
    key_all = add_one(lax.all_gather(wk, "tile", axis=0, tiled=True))
    value_all = add_one(lax.all_gather(wv, "tile", axis=0, tiled=True))
    query_norm = head_norm(query_all, q_gain, count, tokens_tile)
    key_norm = head_norm(key_all, k_gain, count, tokens_tile)
    value_half = value_all.reshape(count, tokens_tile, -1, HD).astype(jnp.bfloat16)
    scores = jnp.einsum(
        "nqhd,nkhd->nhqk", query_norm, key_norm, preferred_element_type=jnp.float32
    ) * HD ** (-0.5)
    peak = jnp.max(scores, axis=-1, keepdims=True)
    expo = jnp.exp(scores - peak)
    probs = (expo / jnp.sum(expo, axis=-1, keepdims=True)).astype(jnp.bfloat16)
    mixed = jnp.einsum("nhqk,nkhd->nqhd", probs, value_half, preferred_element_type=jnp.float32)
    mixed = mixed.astype(jnp.bfloat16).reshape(row_count, -1)
    attn_out = jnp.dot(
        mixed, lax.all_gather(wo, "tile", axis=1, tiled=True), preferred_element_type=jnp.float32
    )
    hidden1 = hidden0 + gate_vec * attn_out
    final = layer_norm(hidden1).astype(jnp.bfloat16)
    eps_pred = jnp.dot(final, out_w, preferred_element_type=jnp.float32).astype(jnp.bfloat16)
    return eps_pred.reshape(count, tokens_tile, token_values)


def on_device(
    latent,
    observed,
    noise,
    cloudy,
    timestep,
    pos_embed,
    embed_w,
    mod_w,
    wq,
    wk,
    wv,
    wo,
    q_gain,
    k_gain,
    out_w,
    conv_w,
):
    channels, band_rows, band_cols = latent.shape
    tile_side = band_rows // PATCH
    tiles_here = band_cols // band_rows
    width = embed_w.shape[1]
    step_now = timestep[0].astype(jnp.float32)
    cos_now, sin_now = plan(step_now)
    cos_prev, sin_prev = plan(step_now - STRIDE)
    time_code = time_features(step_now, mod_w.shape[0])
    local_mod = jnp.dot(time_code, mod_w, preferred_element_type=jnp.float32)
    modulation = lax.all_gather(local_mod, "tile", axis=1, tiled=True)
    shift_vec = modulation[:, :width]
    scale_vec = modulation[:, width : 2 * width]
    gate_vec = modulation[:, 2 * width :]
    tile_tokens = band_tiles(latent.astype(jnp.bfloat16), tile_side)
    order_in = jnp.cumsum(cloudy) - cloudy
    weights_all = (
        embed_w,
        pos_embed,
        shift_vec,
        scale_vec,
        gate_vec,
        wq,
        wk,
        wv,
        wo,
        q_gain,
        k_gain,
        out_w,
    )
    slot_ids = jnp.arange(MAXOWN, dtype=jnp.int32)
    slot_hit = (cloudy[None, :] == 1) & (order_in[None, :] == slot_ids[:, None])
    picked = jnp.sum(
        jnp.where(slot_hit, jnp.arange(tiles_here, dtype=jnp.int32)[None, :], 0), axis=1
    )
    chosen = jnp.take(tile_tokens, picked, axis=0)
    eps_chosen = denoise(chosen, *weights_all)
    eps_back = jnp.take(eps_chosen, jnp.minimum(order_in, MAXOWN - 1), axis=0)
    eps_tiles = jnp.where(cloudy[:, None, None] == 1, eps_back, jnp.zeros_like(eps_back))
    eps_latent = band_pixels(eps_tiles.astype(jnp.float32), tile_side, channels)
    cloud_cols = jnp.repeat(cloudy, band_rows) == 1
    raw_estimate = jnp.where(
        cloud_cols[None, None, :], (latent - sin_now * eps_latent) / cos_now, observed
    )
    padded = padded_2(raw_estimate, (("tile", 1),), 1)
    padded = jnp.pad(padded, ((0, 0), (0, 0), (1, 1)))
    blended = jnp.zeros_like(raw_estimate)
    for row_shift in range(3):
        for col_shift in range(3):
            window = padded[:, row_shift : row_shift + band_rows, col_shift : col_shift + band_cols]
            blended = blended + jnp.einsum(
                "oc,chw->ohw",
                conv_w[3 * row_shift + col_shift],
                window,
                precision=lax.Precision.HIGHEST,
            )
    row_pos = jnp.arange(band_rows) % band_rows
    col_pos = jnp.arange(band_cols) % band_rows
    seam_mask = ((row_pos == 0) | (row_pos == band_rows - 1))[:, None] | (
        (col_pos == 0) | (col_pos == band_rows - 1)
    )[None, :]
    estimate = jnp.where(seam_mask[None], blended, raw_estimate)
    next_latent = cos_prev * estimate + sin_prev * noise
    return (estimate, next_latent)


def solution(mesh):
    placed = (
        P(None, ("grp", "tile"), None),
        P(None, ("grp", "tile"), None),
        P(None, ("grp", "tile"), None),
        P(("grp", "tile")),
        P("grp"),
        P(),
        P(),
        P(None, "tile"),
        P("tile", None),
        P("tile", None),
        P("tile", None),
        P(None, "tile"),
        P(),
        P(),
        P(),
        P(),
    )
    return jax.shard_map(
        on_device,
        mesh=mesh,
        in_specs=placed,
        out_specs=(P(None, ("grp", "tile"), None), P(None, ("grp", "tile"), None)),
        check_vma=False,
    )
```

profile of v0, /device:TPU:1, one launch (start us, length us, event | category | flops | bytes accessed | tf_op | source)
XLA Modules:
  0.0 257.6 jit_solution(8507005595487570797)
XLA Ops:
  12.3 1.1 convolution_bitcast_fusion
  13.6 1.5 copy.77
  15.1 1.1 copy.78
  16.8 1.5 convert_element_type.57
  19.0 23.0 %all-gather.1 = f32[16,1,384]{2,1,0:T(1,128)S(1)} all-gather(f32[1,1,384]{2,1,0:T(1,128)S(1)} %convolution_bitcast_fusion), channel_id=2, replica_groups=mesh['grp'=2,'tile'=16] {'tile'}, dimensions={0}, use_global_device_ids=true | all-gather | bytes 26112 | tf_op jit(solution)/shard_map/all_gather | solution.py:150
  42.1 1.1 fusion.72
  44.0 1.8 copy-done.2
  45.8 2.8 %fusion.4 = bf16[3,256,2048,1]{2,1,3,0:T(8,128)(2,1)} fusion(f32[3,256,2048]{2,1,0:T(8,128)S(1)} %get-tuple-element.22, f32[2048]{0:T(1024)S(1)} %bitcast.119, f32[2048]{0:T(1024)S(1)} %bitcast.118, f32[3,256]{1,0:T(4,128)S(1)} %add_rsqrt_fusion.3, f32[3,256]{1,0:T(4,128)S(1)} %broadcast_multiply_fusion.1), kind=kLoop, calls=%fused_computation.13 | loop fusion | flops 7864320 | bytes 9459712 | tf_op jit(solution)/shard_map/convert_element_type | solution.py:95
  48.7 14.8 %all-gather.11.cloned.1.call-done = bf16[2048,1024]{1,0:T(8,128)(2,1)} async-done(((bf16[128,1024]{1,0:T(8,128)(2,1)}), bf16[2048,1024]{1,0:T(8,128)(2,1)}) %all-gather.11.cloned.1.call-update) | async-done | bytes 4194320 | tf_op jit(solution)/shard_map/all_gather | solution.py:101
  63.5 6.5 %copy.81 = bf16[1024,2048]{1,0:T(8,128)(2,1)} copy(bf16[1024,2048]{0,1:T(8,128)(2,1)} %bitcast.108) | data formatting | bytes 8388608 | tf_op jit(solution)/shard_map/dot_general | solution.py:70
  70.0 44.7 %all-gather.9.cloned.1.call-done = bf16[2048,1024]{1,0:T(8,128)(2,1)} async-done(((bf16[128,1024]{1,0:T(8,128)(2,1)}), bf16[2048,1024]{1,0:T(8,128)(2,1)}) %all-gather.9.cloned.1.call-update) | async-done | bytes 4194320 | tf_op jit(solution)/shard_map/all_gather | solution.py:100
  114.7 6.5 %copy.80 = bf16[1024,2048]{1,0:T(8,128)(2,1)} copy(bf16[1024,2048]{0,1:T(8,128)(2,1)} %bitcast.109) | data formatting | bytes 8388608 | tf_op jit(solution)/shard_map/dot_general | solution.py:70
  121.2 44.7 %all-gather.7.cloned.1.call-done = bf16[2048,1024]{1,0:T(8,128)(2,1)} async-done(((bf16[128,1024]{1,0:T(8,128)(2,1)}), bf16[2048,1024]{1,0:T(8,128)(2,1)}) %all-gather.7.cloned.1.call-update) | async-done | bytes 4194320 | tf_op jit(solution)/shard_map/all_gather | solution.py:102
  166.0 6.5 %copy.79 = bf16[1024,2048]{1,0:T(8,128)(2,1)} copy(bf16[1024,2048]{0,1:T(8,128)(2,1)} %bitcast.110) | data formatting | bytes 8388608 | tf_op jit(solution)/shard_map/dot_general | solution.py:70
  172.4 6.6 %multiply_reduce_fusion.3 = (f32[3,256,8]{1,2,0:T(8,128)S(1)}, f32[3,256,8,128]{1,3,2,0:T(8,128)S(1)}) fusion(bf16[3,256,2048,1]{2,1,3,0:T(8,128)(2,1)} %fusion.4, bf16[8,128,2048,1]{2,1,0,3:T(8,128)(2,1)} %bitcast.113), kind=kOutput, calls=%fused_computation.19 | convolution fusion | flops 3222792192 | bytes 10510336 | tf_op jit(solution)/shard_map/dot_general | solution.py:70
  179.1 3.5 %multiply_reduce_fusion.4 = (f32[3,256,8]{1,2,0:T(8,128)S(1)}, f32[3,256,8,128]{1,3,2,0:T(8,128)S(1)}) fusion(bf16[3,256,2048,1]{2,1,3,0:T(8,128)(2,1)S(1)} %copy-done.4, bf16[8,128,2048,1]{2,1,0,3:T(8,128)(2,1)S(1)} %bitcast.112), kind=kOutput, calls=%fused_computation.21 | convolution fusion | flops 3222792192 | bytes 10510336 | tf_op jit(solution)/shard_map/dot_general | solution.py:70
  182.6 1.3 fusion.11
  183.9 4.3 %fusion.73 = (f32[3,8,256]{2,1,0:T(8,128)S(1)}, f32[3,8,256,256]{2,3,1,0:T(8,128)}) fusion(f32[3,8,256,256]{2,3,1,0:T(8,128)S(1)} %fusion.11), kind=kOutput, calls=%fused_computation.131 | output fusion | flops 6291711 | bytes 12607488 | tf_op jit(solution)/shard_map/sub | solution.py:110
  188.2 10.3 %fusion.18 = bf16[3,256,8,128]{1,3,2,0:T(8,128)(2,1)} fusion(f32[3,8,256,256]{2,3,1,0:T(8,128)} %get-tuple-element.28, f32[3,8,256]{2,1,0:T(8,128)S(1)} %get-tuple-element.27, bf16[3,256,2048,1]{2,1,3,0:T(8,128)(2,1)} %fusion.4, bf16[8,128,2048,1]{2,1,0,3:T(8,128)(2,1)} %bitcast.111), kind=kOutput, calls=%fused_computation.37 | convolution fusion | flops 3628597248 | bytes 15228928 | tf_op jit(solution)/shard_map/nhqk,nkhd->nqhd/dot_general | solution.py:112
  198.5 2.0 copy.86
  200.5 19.2 %all-gather.13.cloned.1.call-done = bf16[1024,2048]{1,0:T(8,128)(2,1)} async-done(((bf16[1024,128]{1,0:T(8,128)(2,1)}), bf16[1024,2048]{1,0:T(8,128)(2,1)}) %all-gather.13.cloned.1.call-update) | async-done | bytes 4194320 | tf_op jit(solution)/shard_map/all_gather | solution.py:115
  219.7 7.0 %fusion.74 = (f32[768]{0:T(1024)S(1)}, f32[768,2048]{1,0:T(8,128)S(1)}) fusion(bf16[1024,2048]{1,0:T(8,128)(2,1)} %all-gather.13.cloned.1.call-done, bf16[96,8,8,128]{3,2,1,0:T(8,128)(2,1)S(1)} %bitcast.115, f32[2048]{0:T(1024)S(1)} %bitcast.120, f32[3,256,2048]{2,1,0:T(8,128)} %copy-done.2), kind=kOutput, calls=%fused_computation.132 | convolution fusion | flops 3225943296 | bytes 18361344 | tf_op jit(solution)/shard_map/dot_general | solution.py:114
  227.8 1.1 fusion.22
  229.9 1.1 multiply_bitcast_fusion
  231.0 1.1 copy.87
  232.7 1.6 copy_select_fusion
  234.4 3.2 %collective-permute-start = (f32[32,1,128]{2,0,1:T(8,128)S(1)}, f32[32,1,128]{2,0,1:T(8,128)S(1)}, u32[]{:S(2)}, u32[]{:S(2)}) collective-permute-start(f32[32,1,128]{2,0,1:T(8,128)S(1)} %get-tuple-element.15), channel_id=1, source_target_pairs={{0,1},{1,2},{2,3},{3,4},{4,5},{5,6},{6,7},{7,8},{8,9},{9,10},{10,1... | collective-permute-start | bytes 49160 | tf_op jit(solution)/shard_map/ppermute | solution.py:19
  237.5 2.2 collective-permute-start.1
  240.0 2.6 %collective-permute-done.1 = f32[32,1,128]{2,0,1:T(8,128)S(1)} collective-permute-done((f32[32,1,128]{2,0,1:T(8,128)S(1)}, f32[32,1,128]{2,0,1:T(8,128)S(1)}, u32[]{:S(2)}, u32[]{:S(2)}) %collective-permute-start.1) | collective-permute-done | bytes 16416 | tf_op jit(solution)/shard_map/ppermute | solution.py:22
  248.0 0.9 fusion.39
  248.9 1.1 copy.92
  250.0 1.1 copy.93
  (69 shorter events, 14.6 us)
Async XLA Ops:
  7.2 34.9 %copy-start = (bf16[128,2048]{1,0:T(8,128)(2,1)S(1)}, bf16[128,2048]{1,0:T(8,128)(2,1)}, u32[]{:S(2)}) copy-start(bf16[128,2048]{1,0:T(8,128)(2,1)} %param.22) | copy-start | bytes 1572868
  7.2 56.3 %all-gather.11.cloned.1.call-start = ((), (), s32[]{:S(2)}) async-start(), calls=%async_computation.2 | async-start | bytes 4456448 | tf_op jit(solution)/shard_map/all_gather | solution.py:101
  7.9 106.8 %all-gather.9.cloned.1.call-start = ((), (), s32[]{:S(2)}) async-start(), calls=%async_computation.1 | async-start | bytes 4456448 | tf_op jit(solution)/shard_map/all_gather | solution.py:100
  8.7 157.3 %all-gather.7.cloned.1.call-start = ((), (), s32[]{:S(2)}) async-start(), calls=%async_computation | async-start | bytes 4456448 | tf_op jit(solution)/shard_map/all_gather | solution.py:102
  9.4 210.3 %all-gather.13.cloned.1.call-start = ((), (), s32[]{:S(2)}) async-start(), calls=%async_computation.3 | async-start | bytes 4456448 | tf_op jit(solution)/shard_map/all_gather | solution.py:115
  43.2 2.7 %copy-start.2 = (f32[3,256,2048]{2,1,0:T(8,128)}, f32[3,256,2048]{2,1,0:T(8,128)S(1)}, u32[]{:S(2)}) copy-start(f32[3,256,2048]{2,1,0:T(8,128)S(1)} %get-tuple-element.22) | copy-start | bytes 18874372
  172.4 6.7 %copy-start.3 = (bf16[1024,2048]{1,0:T(8,128)(2,1)S(1)}, bf16[1024,2048]{1,0:T(8,128)(2,1)}, u32[]{:S(2)}) copy-start(bf16[1024,2048]{1,0:T(8,128)(2,1)} %copy.80) | copy-start | bytes 12582916
  172.4 6.7 %copy-start.4 = (bf16[3,256,2048,1]{2,1,3,0:T(8,128)(2,1)S(1)}, bf16[3,256,2048,1]{2,1,3,0:T(8,128)(2,1)}, u32[]{:S(2)}) copy-start(bf16[3,256,2048,1]{2,1,3,0:T(8,128)(2,1)} %fusion.4) | copy-start | bytes 9437188
  179.1 3.5 %copy-start.9 = (f32[128]{0:T(128)S(1)}, f32[128]{0:T(128)}, u32[]{:S(2)}) copy-start(f32[128]{0:T(128)} %param.29) | copy-start | bytes 1540
  179.1 3.5 %copy-start.10 = (f32[128]{0:T(128)S(1)}, f32[128]{0:T(128)}, u32[]{:S(2)}) copy-start(f32[128]{0:T(128)} %param.28) | copy-start | bytes 1540
  226.7 1.0 copy-start.7
  230.9 1.8 copy-start.5
  232.1 10.8 %copy-start.8 = (f32[9,32,32]{2,1,0:T(8,128)S(1)}, f32[9,32,32]{2,1,0:T(8,128)}, u32[]{:S(2)}) copy-start(f32[9,32,32]{2,1,0:T(8,128)} %param.31) | copy-start | bytes 110596
  234.4 5.6 %collective-permute-start = (f32[32,1,128]{2,0,1:T(8,128)S(1)}, f32[32,1,128]{2,0,1:T(8,128)S(1)}, u32[]{:S(2)}, u32[]{:S(2)}) collective-permute-start(f32[32,1,128]{2,0,1:T(8,128)S(1)} %get-tuple-element.15), channel_id=1, source_target_pairs={{0,1},{1,2},{2,3},{3,4},{4,5},{5,6},{6,7},{7,8},{8,9},{9,10},{10,1... | collective-permute-start | bytes 49160 | tf_op jit(solution)/shard_map/ppermute | solution.py:19
  237.5 5.1 %collective-permute-start.1 = (f32[32,1,128]{2,0,1:T(8,128)S(1)}, f32[32,1,128]{2,0,1:T(8,128)S(1)}, u32[]{:S(2)}, u32[]{:S(2)}) collective-permute-start(f32[32,1,128]{2,0,1:T(8,128)S(1)} %get-tuple-element.16), channel_id=1, source_target_pairs={{1,0},{2,1},{3,2},{4,3},{5,4},{6,5},{7,6},{8,7},{9,8},{10,9},{11,1... | collective-permute-start | bytes 49160 | tf_op jit(solution)/shard_map/ppermute | solution.py:22
  245.5 2.5 copy-start.6
  247.4 3.7 %copy-start.1 = (bf16[128,2048]{1,0:T(8,128)(2,1)S(1)}, bf16[128,2048]{1,0:T(8,128)(2,1)}, u32[]{:S(2)}) copy-start(bf16[128,2048]{1,0:T(8,128)(2,1)} %param.22) | copy-start | bytes 1572868
Sparse Core Ops, SparseCore 0:
  10.2 53.2 all-gather.10
  65.6 49.0 all-gather.8
  116.9 49.0 all-gather.6
  168.0 51.7 all-gather.12
where the time goes:
time: 258 us
  waiting for transfers between devices  129 us (50%)
  matrix products  37.7 us (15%)
  local copies, waits for them, and re-layouts  32.5 us (13%)
  blocking collectives  23 us (9%)
  between operations  15.2 us (6%)
  other arithmetic  15 us (6%)
  starting transfers between devices  5.5 us (2%)
    all_gather x1, waiting for transfers between devices, denoise(): value_all = add_one(lax.all_gather(wv, 'tile', axis=0, tiled=True))  44.7 us
    all_gather x1, waiting for transfers between devices, denoise(): query_all = add_one(lax.all_gather(wq, 'tile', axis=0, tiled=True))  44.7 us
    all_gather x1, blocking collectives, on_device(): modulation = lax.all_gather(local_mod, 'tile', axis=1, tiled=True)  23 us
    dot_general x3, local copies, waits for them, and re-layouts, add_rows(): return jnp.dot(left, shard_rows, preferred_element_type=jnp.float32)  19.5 us
    all_gather x1, waiting for transfers between devices, denoise(): lax.all_gather(wo, 'tile', axis=1, tiled=True)  19.2 us
    all_gather x1, waiting for transfers between devices, denoise(): key_all = add_one(lax.all_gather(wk, 'tile', axis=0, tiled=True))  14.8 us
    dot_general x1, matrix products, denoise(): jnp.einsum('nhqk,nkhd->nqhd', probs, value_half, preferred_element_type=j...  10.3 us
    dot_general x2, matrix products, add_rows(): return jnp.dot(left, shard_rows, preferred_element_type=jnp.float32)  10.1 us
  transfers between devices with their start and end apart: 6, of which 5 were waited for; matrix products, arithmetic and copies ran while one was open for 23% of the time, Pallas kernels for 0%

commit v1 on v0

--- a/solution.py
+++ b/solution.py
@@ -147,7 +147,12 @@
     cos_prev, sin_prev = plan(step_now - STRIDE)
     time_code = time_features(step_now, mod_w.shape[0])
     local_mod = jnp.dot(time_code, mod_w, preferred_element_type=jnp.float32)
-    modulation = lax.all_gather(local_mod, "tile", axis=1, tiled=True)
+    ring = [local_mod]
+    for hop in range(15):
+        ring.append(lax.ppermute(ring[-1], "tile", [(dev, (dev + 1) % 16) for dev in range(16)]))
+    modulation = jnp.roll(
+        jnp.concatenate(ring[::-1], axis=1), (lax.axis_index("tile") + 1) * ring[0].shape[1], axis=1
+    )
     shift_vec = modulation[:, :width]
     scale_vec = modulation[:, width : 2 * width]
     gate_vec = modulation[:, 2 * width :]

time: 258 us -> 258 us (level)
  blocking collectives: 23 us -> 0 us
  waiting for transfers between devices: 129 us -> 144 us
  starting transfers between devices: 5.5 us -> 11.7 us
  other arithmetic: 15 us -> 18 us
    ppermute x0 -> x15, waiting for transfers between devices: none -> 66.6 us  [on_device(): lax.ppermute(ring[-1], 'tile', [(dev, (dev + 1) % 16) for dev in range(16)])]
    all_gather x1, waiting for transfers between devices: 44.7 us -> 8.64 us  [denoise(): query_all = add_one(lax.all_gather(wq, 'tile', axis=0, tiled=True))]
    all_gather x1 -> x0, blocking collectives: 23 us -> none  [on_device(): modulation = lax.all_gather(local_mod, 'tile', axis=1, tiled=True)]
    all_gather x1, waiting for transfers between devices: 14.8 us -> 0.01 us  [denoise(): key_all = add_one(lax.all_gather(wk, 'tile', axis=0, tiled=True))]
    ppermute x0 -> x15, starting transfers between devices: none -> 6.17 us  [on_device(): lax.ppermute(ring[-1], 'tile', [(dev, (dev + 1) % 16) for dev in range(16)])]
    convert_element_type x1, other arithmetic: 2.83 us -> 5.69 us  [denoise(): (layer_norm(hidden0) * (1.0 + scale_vec) + shift_vec).astype(jnp.bfloat16)]
    unnamed x25 -> x56, local copies, waits for them, and re-layouts: 5.88 us -> 4.31 us
  transfers between devices with their start and end apart: 6 -> 21, of which waited for: 5 -> 19; matrix products, arithmetic and copies ran while one was open for 23% -> 25% of each run, Pallas kernels for 0% -> 0%
where the time goes in v1:
time: 258 us; the launch traced here: 257 us
  waiting for transfers between devices  144 us (56%)
  matrix products  37.7 us (15%)
  local copies, waits for them, and re-layouts  31 us (12%)
  other arithmetic  18 us (7%)
  between operations  15.3 us (6%)
  starting transfers between devices  11.7 us (5%)
    ppermute x15, waiting for transfers between devices, on_device(): lax.ppermute(ring[-1], 'tile', [(dev, (dev + 1) % 16) for dev in range(16)])  66.6 us
    all_gather x1, waiting for transfers between devices, denoise(): value_all = add_one(lax.all_gather(wv, 'tile', axis=0, tiled=True))  44.7 us
    dot_general x3, local copies, waits for them, and re-layouts, add_rows(): return jnp.dot(left, shard_rows, preferred_element_type=jnp.float32)  19.5 us
    all_gather x1, waiting for transfers between devices, denoise(): lax.all_gather(wo, 'tile', axis=1, tiled=True)  19.3 us
    dot_general x1, matrix products, denoise(): jnp.einsum('nhqk,nkhd->nqhd', probs, value_half, preferred_element_type=j...  10.3 us
    dot_general x2, matrix products, add_rows(): return jnp.dot(left, shard_rows, preferred_element_type=jnp.float32)  10.1 us
    all_gather x1, waiting for transfers between devices, denoise(): query_all = add_one(lax.all_gather(wq, 'tile', axis=0, tiled=True))  8.64 us
    dot_general x1, matrix products, denoise(): jnp.dot(mixed, lax.all_gather(wo, 'tile', axis=1, tiled=True), preferred_...  6.98 us
  transfers between devices with their start and end apart: 21, of which 19 were waited for; matrix products, arithmetic and copies ran while one was open for 25% of the time, Pallas kernels for 0%

profile of v1, /device:TPU:1, one launch (start us, length us, event | category | flops | bytes accessed | tf_op | source)
XLA Modules:
  0.0 257.5 jit_solution(2343788766092399168)
XLA Ops:
  11.2 2.6 %collective-permute-start = (f32[1,384]{1,0:T(1,128)S(1)}, f32[1,384]{1,0:T(1,128)S(1)}, u32[]{:S(2)}, u32[]{:S(2)}) collective-permute-start(f32[1,384]{1,0:T(1,128)S(1)} %fusion.78), channel_id=1, source_target_pairs={{0,1},{1,2},{2,3},{3,4},{4,5},{5,6},{6,7},{7,8},{8,9},{9,10},{10,1... | collective-permute-start | bytes 4616 | tf_op jit(solution)/shard_map/ppermute | solution.py:152
  14.6 2.3 collective-permute-start.1
  16.9 1.8 collective-permute-done.1
  20.7 3.7 %collective-permute-done.2 = f32[1,384]{1,0:T(1,128)S(1)} collective-permute-done((f32[1,384]{1,0:T(1,128)S(1)}, f32[1,384]{1,0:T(1,128)S(1)}, u32[]{:S(2)}, u32[]{:S(2)}) %collective-permute-start.2) | collective-permute-done | bytes 1568 | tf_op jit(solution)/shard_map/ppermute | solution.py:152
  25.1 5.0 %collective-permute-done.3 = f32[1,384]{1,0:T(1,128)S(1)} collective-permute-done((f32[1,384]{1,0:T(1,128)S(1)}, f32[1,384]{1,0:T(1,128)S(1)}, u32[]{:S(2)}, u32[]{:S(2)}) %collective-permute-start.3) | collective-permute-done | bytes 1568 | tf_op jit(solution)/shard_map/ppermute | solution.py:152
  30.3 5.6 %collective-permute-done.4 = f32[1,384]{1,0:T(1,128)S(1)} collective-permute-done((f32[1,384]{1,0:T(1,128)S(1)}, f32[1,384]{1,0:T(1,128)S(1)}, u32[]{:S(2)}, u32[]{:S(2)}) %collective-permute-start.4) | collective-permute-done | bytes 1568 | tf_op jit(solution)/shard_map/ppermute | solution.py:152
  35.9 5.7 %collective-permute-done.5 = f32[1,384]{1,0:T(1,128)S(1)} collective-permute-done((f32[1,384]{1,0:T(1,128)S(1)}, f32[1,384]{1,0:T(1,128)S(1)}, u32[]{:S(2)}, u32[]{:S(2)}) %collective-permute-start.5) | collective-permute-done | bytes 1568 | tf_op jit(solution)/shard_map/ppermute | solution.py:152
  41.6 5.8 %collective-permute-done.6 = f32[1,384]{1,0:T(1,128)S(1)} collective-permute-done((f32[1,384]{1,0:T(1,128)S(1)}, f32[1,384]{1,0:T(1,128)S(1)}, u32[]{:S(2)}, u32[]{:S(2)}) %collective-permute-start.6) | collective-permute-done | bytes 1568 | tf_op jit(solution)/shard_map/ppermute | solution.py:152
  54.3 4.6 %collective-permute-done.8 = f32[1,384]{1,0:T(1,128)S(1)} collective-permute-done((f32[1,384]{1,0:T(1,128)S(1)}, f32[1,384]{1,0:T(1,128)S(1)}, u32[]{:S(2)}, u32[]{:S(2)}) %collective-permute-start.8) | collective-permute-done | bytes 1568 | tf_op jit(solution)/shard_map/ppermute | solution.py:152
  58.9 5.7 %collective-permute-done.9 = f32[1,384]{1,0:T(1,128)S(1)} collective-permute-done((f32[1,384]{1,0:T(1,128)S(1)}, f32[1,384]{1,0:T(1,128)S(1)}, u32[]{:S(2)}, u32[]{:S(2)}) %collective-permute-start.9) | collective-permute-done | bytes 1568 | tf_op jit(solution)/shard_map/ppermute | solution.py:152
  65.4 4.9 %collective-permute-done.10 = f32[1,384]{1,0:T(1,128)S(1)} collective-permute-done((f32[1,384]{1,0:T(1,128)S(1)}, f32[1,384]{1,0:T(1,128)S(1)}, u32[]{:S(2)}, u32[]{:S(2)}) %collective-permute-start.10) | collective-permute-done | bytes 1568 | tf_op jit(solution)/shard_map/ppermute | solution.py:152
  70.3 5.8 %collective-permute-done.11 = f32[1,384]{1,0:T(1,128)S(1)} collective-permute-done((f32[1,384]{1,0:T(1,128)S(1)}, f32[1,384]{1,0:T(1,128)S(1)}, u32[]{:S(2)}, u32[]{:S(2)}) %collective-permute-start.11) | collective-permute-done | bytes 1568 | tf_op jit(solution)/shard_map/ppermute | solution.py:152
  76.1 5.7 %collective-permute-done.12 = f32[1,384]{1,0:T(1,128)S(1)} collective-permute-done((f32[1,384]{1,0:T(1,128)S(1)}, f32[1,384]{1,0:T(1,128)S(1)}, u32[]{:S(2)}, u32[]{:S(2)}) %collective-permute-start.12) | collective-permute-done | bytes 1568 | tf_op jit(solution)/shard_map/ppermute | solution.py:152
  81.8 5.7 %collective-permute-done.13 = f32[1,384]{1,0:T(1,128)S(1)} collective-permute-done((f32[1,384]{1,0:T(1,128)S(1)}, f32[1,384]{1,0:T(1,128)S(1)}, u32[]{:S(2)}, u32[]{:S(2)}) %collective-permute-start.13) | collective-permute-done | bytes 1568 | tf_op jit(solution)/shard_map/ppermute | solution.py:152
  87.9 5.4 %collective-permute-done.14 = f32[1,384]{1,0:T(1,128)S(1)} collective-permute-done((f32[1,384]{1,0:T(1,128)S(1)}, f32[1,384]{1,0:T(1,128)S(1)}, u32[]{:S(2)}, u32[]{:S(2)}) %collective-permute-start.14) | collective-permute-done | bytes 1568 | tf_op jit(solution)/shard_map/ppermute | solution.py:152
  93.7 5.7 %fusion.4 = bf16[3,256,2048,1]{2,1,3,0:T(8,128)(2,1)} fusion(f32[3,256,2048]{2,1,0:T(8,128)} %copy-done.2, f32[2048]{0:T(1024)S(1)} %bitcast.117, f32[2048]{0:T(1024)S(1)} %bitcast.116, f32[3,256]{1,0:T(4,128)S(1)} %add_rsqrt_fusion.3, f32[3,256]{1,0:T(4,128)S(1)} %broadcast_multiply_fusion.1), kind=kLoop, calls=%fused_computation.13 | loop fusion | flops 7864320 | bytes 9459712 | tf_op jit(solution)/shard_map/convert_element_type | solution.py:95
  99.4 6.5 %copy.64 = bf16[1024,2048]{1,0:T(8,128)(2,1)} copy(bf16[1024,2048]{0,1:T(8,128)(2,1)} %bitcast.107) | data formatting | bytes 8388608 | tf_op jit(solution)/shard_map/dot_general | solution.py:70
  105.9 8.6 %all-gather.7.cloned.1.call-done = bf16[2048,1024]{1,0:T(8,128)(2,1)} async-done(((bf16[128,1024]{1,0:T(8,128)(2,1)}), bf16[2048,1024]{1,0:T(8,128)(2,1)}) %all-gather.7.cloned.1.call-update) | async-done | bytes 4194320 | tf_op jit(solution)/shard_map/all_gather | solution.py:100
  114.6 6.6 %copy.63 = bf16[1024,2048]{1,0:T(8,128)(2,1)} copy(bf16[1024,2048]{0,1:T(8,128)(2,1)} %bitcast.108) | data formatting | bytes 8388608 | tf_op jit(solution)/shard_map/dot_general | solution.py:70
  121.1 44.7 %all-gather.5.cloned.1.call-done = bf16[2048,1024]{1,0:T(8,128)(2,1)} async-done(((bf16[128,1024]{1,0:T(8,128)(2,1)}), bf16[2048,1024]{1,0:T(8,128)(2,1)}) %all-gather.5.cloned.1.call-update) | async-done | bytes 4194320 | tf_op jit(solution)/shard_map/all_gather | solution.py:102
  165.8 6.5 %copy.62 = bf16[1024,2048]{1,0:T(8,128)(2,1)} copy(bf16[1024,2048]{0,1:T(8,128)(2,1)} %bitcast.109) | data formatting | bytes 8388608 | tf_op jit(solution)/shard_map/dot_general | solution.py:70
  172.3 6.6 %multiply_reduce_fusion.3 = (f32[3,256,8]{1,2,0:T(8,128)S(1)}, f32[3,256,8,128]{1,3,2,0:T(8,128)S(1)}) fusion(bf16[3,256,2048,1]{2,1,3,0:T(8,128)(2,1)} %fusion.4, bf16[8,128,2048,1]{2,1,0,3:T(8,128)(2,1)} %bitcast.112), kind=kOutput, calls=%fused_computation.19 | convolution fusion | flops 3222792192 | bytes 10510336 | tf_op jit(solution)/shard_map/dot_general | solution.py:70
  179.0 3.5 %multiply_reduce_fusion.4 = (f32[3,256,8]{1,2,0:T(8,128)S(1)}, f32[3,256,8,128]{1,3,2,0:T(8,128)S(1)}) fusion(bf16[3,256,2048,1]{2,1,3,0:T(8,128)(2,1)S(1)} %copy-done.4, bf16[8,128,2048,1]{2,1,0,3:T(8,128)(2,1)S(1)} %bitcast.111), kind=kOutput, calls=%fused_computation.21 | convolution fusion | flops 3222792192 | bytes 10510336 | tf_op jit(solution)/shard_map/dot_general | solution.py:70
  183.8 4.3 %fusion.76 = (f32[3,8,256]{2,1,0:T(8,128)S(1)}, f32[3,8,256,256]{2,3,1,0:T(8,128)}) fusion(f32[3,8,256,256]{2,3,1,0:T(8,128)S(1)} %fusion.11), kind=kOutput, calls=%fused_computation.165 | output fusion | flops 6291711 | bytes 12607488 | tf_op jit(solution)/shard_map/sub | solution.py:110
  188.1 10.3 %fusion.21 = bf16[3,256,8,128]{1,3,2,0:T(8,128)(2,1)} fusion(f32[3,8,256,256]{2,3,1,0:T(8,128)} %get-tuple-element.26, f32[3,8,256]{2,1,0:T(8,128)S(1)} %get-tuple-element.25, bf16[3,256,2048,1]{2,1,3,0:T(8,128)(2,1)} %fusion.4, bf16[8,128,2048,1]{2,1,0,3:T(8,128)(2,1)} %bitcast.110), kind=kOutput, calls=%fused_computation.38 | convolution fusion | flops 3628597248 | bytes 15228928 | tf_op jit(solution)/shard_map/nhqk,nkhd->nqhd/dot_general | solution.py:112
  198.3 2.0 copy.69
  200.3 19.3 %all-gather.11.cloned.1.call-done = bf16[1024,2048]{1,0:T(8,128)(2,1)} async-done(((bf16[1024,128]{1,0:T(8,128)(2,1)}), bf16[1024,2048]{1,0:T(8,128)(2,1)}) %all-gather.11.cloned.1.call-update) | async-done | bytes 4194320 | tf_op jit(solution)/shard_map/all_gather | solution.py:115
  219.6 7.0 %fusion.77 = (f32[768]{0:T(1024)S(1)}, f32[768,2048]{1,0:T(8,128)S(1)}) fusion(bf16[1024,2048]{1,0:T(8,128)(2,1)} %all-gather.11.cloned.1.call-done, bf16[96,8,8,128]{3,2,1,0:T(8,128)(2,1)S(1)} %bitcast.114, f32[2048]{0:T(1024)S(1)} %bitcast.118, f32[3,256,2048]{2,1,0:T(8,128)} %copy-done.2), kind=kOutput, calls=%fused_computation.166 | convolution fusion | flops 3225943296 | bytes 18361344 | tf_op jit(solution)/shard_map/dot_general | solution.py:114
  232.6 1.6 copy_select_fusion
  234.2 3.2 %collective-permute-start.15 = (f32[32,1,128]{2,0,1:T(8,128)S(1)}, f32[32,1,128]{2,0,1:T(8,128)S(1)}, u32[]{:S(2)}, u32[]{:S(2)}) collective-permute-start(f32[32,1,128]{2,0,1:T(8,128)S(1)} %get-tuple-element.13), channel_id=1, source_target_pairs={{0,1},{1,2},{2,3},{3,4},{4,5},{5,6},{6,7},{7,8},{8,9},{9,10},{10,1... | collective-permute-start | bytes 49160 | tf_op jit(solution)/shard_map/ppermute | solution.py:19
  237.4 2.2 collective-permute-start.16
  239.8 2.6 %collective-permute-done.16 = f32[32,1,128]{2,0,1:T(8,128)S(1)} collective-permute-done((f32[32,1,128]{2,0,1:T(8,128)S(1)}, f32[32,1,128]{2,0,1:T(8,128)S(1)}, u32[]{:S(2)}, u32[]{:S(2)}) %collective-permute-start.16) | collective-permute-done | bytes 16416 | tf_op jit(solution)/shard_map/ppermute | solution.py:22
  (129 shorter events, 30.9 us)
Async XLA Ops:
  7.2 46.0 %copy-start = (bf16[128,2048]{1,0:T(8,128)(2,1)S(1)}, bf16[128,2048]{1,0:T(8,128)(2,1)}, u32[]{:S(2)}) copy-start(bf16[128,2048]{1,0:T(8,128)(2,1)} %param.22) | copy-start | bytes 1572868
  7.2 92.2 %all-gather.9.cloned.1.call-start = ((), (), s32[]{:S(2)}) async-start(), calls=%async_computation.2 | async-start | bytes 4456448 | tf_op jit(solution)/shard_map/all_gather | solution.py:101
  7.9 106.6 %all-gather.7.cloned.1.call-start = ((), (), s32[]{:S(2)}) async-start(), calls=%async_computation.1 | async-start | bytes 4456448 | tf_op jit(solution)/shard_map/all_gather | solution.py:100
  8.7 157.2 %all-gather.5.cloned.1.call-start = ((), (), s32[]{:S(2)}) async-start(), calls=%async_computation | async-start | bytes 4456448 | tf_op jit(solution)/shard_map/all_gather | solution.py:102
  9.4 210.2 %all-gather.11.cloned.1.call-start = ((), (), s32[]{:S(2)}) async-start(), calls=%async_computation.3 | async-start | bytes 4456448 | tf_op jit(solution)/shard_map/all_gather | solution.py:115
  11.2 3.4 %collective-permute-start = (f32[1,384]{1,0:T(1,128)S(1)}, f32[1,384]{1,0:T(1,128)S(1)}, u32[]{:S(2)}, u32[]{:S(2)}) collective-permute-start(f32[1,384]{1,0:T(1,128)S(1)} %fusion.78), channel_id=1, source_target_pairs={{0,1},{1,2},{2,3},{3,4},{4,5},{5,6},{6,7},{7,8},{8,9},{9,10},{10,1... | collective-permute-start | bytes 4616 | tf_op jit(solution)/shard_map/ppermute | solution.py:152
  14.6 4.0 %collective-permute-start.1 = (f32[1,384]{1,0:T(1,128)S(1)}, f32[1,384]{1,0:T(1,128)S(1)}, u32[]{:S(2)}, u32[]{:S(2)}) collective-permute-start(f32[1,384]{1,0:T(1,128)S(1)} %collective-permute-done), channel_id=1, source_target_pairs={{0,1},{1,2},{2,3},{3,4},{4,5},{5,6},{6,7},{7,8},{8,9},{9,10},{10,1... | collective-permute-start | bytes 4616 | tf_op jit(solution)/shard_map/ppermute | solution.py:152
  18.7 5.8 %collective-permute-start.2 = (f32[1,384]{1,0:T(1,128)S(1)}, f32[1,384]{1,0:T(1,128)S(1)}, u32[]{:S(2)}, u32[]{:S(2)}) collective-permute-start(f32[1,384]{1,0:T(1,128)S(1)} %collective-permute-done.1), channel_id=1, source_target_pairs={{0,1},{1,2},{2,3},{3,4},{4,5},{5,6},{6,7},{7,8},{8,9},{9,10},{10,1... | collective-permute-start | bytes 4616 | tf_op jit(solution)/shard_map/ppermute | solution.py:152
  24.5 5.7 %collective-permute-start.3 = (f32[1,384]{1,0:T(1,128)S(1)}, f32[1,384]{1,0:T(1,128)S(1)}, u32[]{:S(2)}, u32[]{:S(2)}) collective-permute-start(f32[1,384]{1,0:T(1,128)S(1)} %collective-permute-done.2), channel_id=1, source_target_pairs={{0,1},{1,2},{2,3},{3,4},{4,5},{5,6},{6,7},{7,8},{8,9},{9,10},{10,1... | collective-permute-start | bytes 4616 | tf_op jit(solution)/shard_map/ppermute | solution.py:152
  30.2 5.7 %collective-permute-start.4 = (f32[1,384]{1,0:T(1,128)S(1)}, f32[1,384]{1,0:T(1,128)S(1)}, u32[]{:S(2)}, u32[]{:S(2)}) collective-permute-start(f32[1,384]{1,0:T(1,128)S(1)} %collective-permute-done.3), channel_id=1, source_target_pairs={{0,1},{1,2},{2,3},{3,4},{4,5},{5,6},{6,7},{7,8},{8,9},{9,10},{10,1... | collective-permute-start | bytes 4616 | tf_op jit(solution)/shard_map/ppermute | solution.py:152
  35.9 5.7 %collective-permute-start.5 = (f32[1,384]{1,0:T(1,128)S(1)}, f32[1,384]{1,0:T(1,128)S(1)}, u32[]{:S(2)}, u32[]{:S(2)}) collective-permute-start(f32[1,384]{1,0:T(1,128)S(1)} %collective-permute-done.4), channel_id=1, source_target_pairs={{0,1},{1,2},{2,3},{3,4},{4,5},{5,6},{6,7},{7,8},{8,9},{9,10},{10,1... | collective-permute-start | bytes 4616 | tf_op jit(solution)/shard_map/ppermute | solution.py:152
  41.6 5.8 %collective-permute-start.6 = (f32[1,384]{1,0:T(1,128)S(1)}, f32[1,384]{1,0:T(1,128)S(1)}, u32[]{:S(2)}, u32[]{:S(2)}) collective-permute-start(f32[1,384]{1,0:T(1,128)S(1)} %collective-permute-done.5), channel_id=1, source_target_pairs={{0,1},{1,2},{2,3},{3,4},{4,5},{5,6},{6,7},{7,8},{8,9},{9,10},{10,1... | collective-permute-start | bytes 4616 | tf_op jit(solution)/shard_map/ppermute | solution.py:152
  47.4 5.8 %collective-permute-start.7 = (f32[1,384]{1,0:T(1,128)S(1)}, f32[1,384]{1,0:T(1,128)S(1)}, u32[]{:S(2)}, u32[]{:S(2)}) collective-permute-start(f32[1,384]{1,0:T(1,128)S(1)} %collective-permute-done.6), channel_id=1, source_target_pairs={{0,1},{1,2},{2,3},{3,4},{4,5},{5,6},{6,7},{7,8},{8,9},{9,10},{10,1... | collective-permute-start | bytes 4616 | tf_op jit(solution)/shard_map/ppermute | solution.py:152
  53.2 5.7 %collective-permute-start.8 = (f32[1,384]{1,0:T(1,128)S(1)}, f32[1,384]{1,0:T(1,128)S(1)}, u32[]{:S(2)}, u32[]{:S(2)}) collective-permute-start(f32[1,384]{1,0:T(1,128)S(1)} %collective-permute-done.7), channel_id=1, source_target_pairs={{0,1},{1,2},{2,3},{3,4},{4,5},{5,6},{6,7},{7,8},{8,9},{9,10},{10,1... | collective-permute-start | bytes 4616 | tf_op jit(solution)/shard_map/ppermute | solution.py:152
  54.3 11.1 %copy-start.2 = (f32[3,256,2048]{2,1,0:T(8,128)}, f32[3,256,2048]{2,1,0:T(8,128)S(1)}, u32[]{:S(2)}) copy-start(f32[3,256,2048]{2,1,0:T(8,128)S(1)} %get-tuple-element.20) | copy-start | bytes 18874372
  58.9 5.7 %collective-permute-start.9 = (f32[1,384]{1,0:T(1,128)S(1)}, f32[1,384]{1,0:T(1,128)S(1)}, u32[]{:S(2)}, u32[]{:S(2)}) collective-permute-start(f32[1,384]{1,0:T(1,128)S(1)} %collective-permute-done.8), channel_id=1, source_target_pairs={{0,1},{1,2},{2,3},{3,4},{4,5},{5,6},{6,7},{7,8},{8,9},{9,10},{10,1... | collective-permute-start | bytes 4616 | tf_op jit(solution)/shard_map/ppermute | solution.py:152
  64.6 5.7 %collective-permute-start.10 = (f32[1,384]{1,0:T(1,128)S(1)}, f32[1,384]{1,0:T(1,128)S(1)}, u32[]{:S(2)}, u32[]{:S(2)}) collective-permute-start(f32[1,384]{1,0:T(1,128)S(1)} %collective-permute-done.9), channel_id=1, source_target_pairs={{0,1},{1,2},{2,3},{3,4},{4,5},{5,6},{6,7},{7,8},{8,9},{9,10},{10,1... | collective-permute-start | bytes 4616 | tf_op jit(solution)/shard_map/ppermute | solution.py:152
  70.3 5.8 %collective-permute-start.11 = (f32[1,384]{1,0:T(1,128)S(1)}, f32[1,384]{1,0:T(1,128)S(1)}, u32[]{:S(2)}, u32[]{:S(2)}) collective-permute-start(f32[1,384]{1,0:T(1,128)S(1)} %collective-permute-done.10), channel_id=1, source_target_pairs={{0,1},{1,2},{2,3},{3,4},{4,5},{5,6},{6,7},{7,8},{8,9},{9,10},{10,1... | collective-permute-start | bytes 4616 | tf_op jit(solution)/shard_map/ppermute | solution.py:152
  76.1 5.7 %collective-permute-start.12 = (f32[1,384]{1,0:T(1,128)S(1)}, f32[1,384]{1,0:T(1,128)S(1)}, u32[]{:S(2)}, u32[]{:S(2)}) collective-permute-start(f32[1,384]{1,0:T(1,128)S(1)} %collective-permute-done.11), channel_id=1, source_target_pairs={{0,1},{1,2},{2,3},{3,4},{4,5},{5,6},{6,7},{7,8},{8,9},{9,10},{10,1... | collective-permute-start | bytes 4616 | tf_op jit(solution)/shard_map/ppermute | solution.py:152
  81.8 5.7 %collective-permute-start.13 = (f32[1,384]{1,0:T(1,128)S(1)}, f32[1,384]{1,0:T(1,128)S(1)}, u32[]{:S(2)}, u32[]{:S(2)}) collective-permute-start(f32[1,384]{1,0:T(1,128)S(1)} %collective-permute-done.12), channel_id=1, source_target_pairs={{0,1},{1,2},{2,3},{3,4},{4,5},{5,6},{6,7},{7,8},{8,9},{9,10},{10,1... | collective-permute-start | bytes 4616 | tf_op jit(solution)/shard_map/ppermute | solution.py:152
  87.5 5.7 %collective-permute-start.14 = (f32[1,384]{1,0:T(1,128)S(1)}, f32[1,384]{1,0:T(1,128)S(1)}, u32[]{:S(2)}, u32[]{:S(2)}) collective-permute-start(f32[1,384]{1,0:T(1,128)S(1)} %collective-permute-done.13), channel_id=1, source_target_pairs={{0,1},{1,2},{2,3},{3,4},{4,5},{5,6},{6,7},{7,8},{8,9},{9,10},{10,1... | collective-permute-start | bytes 4616 | tf_op jit(solution)/shard_map/ppermute | solution.py:152
  172.3 6.7 %copy-start.3 = (bf16[1024,2048]{1,0:T(8,128)(2,1)S(1)}, bf16[1024,2048]{1,0:T(8,128)(2,1)}, u32[]{:S(2)}) copy-start(bf16[1024,2048]{1,0:T(8,128)(2,1)} %copy.63) | copy-start | bytes 12582916
  172.3 6.7 %copy-start.4 = (bf16[3,256,2048,1]{2,1,3,0:T(8,128)(2,1)S(1)}, bf16[3,256,2048,1]{2,1,3,0:T(8,128)(2,1)}, u32[]{:S(2)}) copy-start(bf16[3,256,2048,1]{2,1,3,0:T(8,128)(2,1)} %fusion.4) | copy-start | bytes 9437188
  178.9 3.5 %copy-start.9 = (f32[128]{0:T(128)S(1)}, f32[128]{0:T(128)}, u32[]{:S(2)}) copy-start(f32[128]{0:T(128)} %param.29) | copy-start | bytes 1540
  179.0 3.5 %copy-start.10 = (f32[128]{0:T(128)S(1)}, f32[128]{0:T(128)}, u32[]{:S(2)}) copy-start(f32[128]{0:T(128)} %param.28) | copy-start | bytes 1540
  226.6 1.0 copy-start.7
  230.8 1.8 copy-start.5
  232.0 10.8 %copy-start.8 = (f32[9,32,32]{2,1,0:T(8,128)S(1)}, f32[9,32,32]{2,1,0:T(8,128)}, u32[]{:S(2)}) copy-start(f32[9,32,32]{2,1,0:T(8,128)} %param.31) | copy-start | bytes 110596
  234.2 5.6 %collective-permute-start.15 = (f32[32,1,128]{2,0,1:T(8,128)S(1)}, f32[32,1,128]{2,0,1:T(8,128)S(1)}, u32[]{:S(2)}, u32[]{:S(2)}) collective-permute-start(f32[32,1,128]{2,0,1:T(8,128)S(1)} %get-tuple-element.13), channel_id=1, source_target_pairs={{0,1},{1,2},{2,3},{3,4},{4,5},{5,6},{6,7},{7,8},{8,9},{9,10},{10,1... | collective-permute-start | bytes 49160 | tf_op jit(solution)/shard_map/ppermute | solution.py:19
  237.4 5.1 %collective-permute-start.16 = (f32[32,1,128]{2,0,1:T(8,128)S(1)}, f32[32,1,128]{2,0,1:T(8,128)S(1)}, u32[]{:S(2)}, u32[]{:S(2)}) collective-permute-start(f32[32,1,128]{2,0,1:T(8,128)S(1)} %get-tuple-element.14), channel_id=1, source_target_pairs={{1,0},{2,1},{3,2},{4,3},{5,4},{6,5},{7,6},{8,7},{9,8},{10,9},{11,1... | collective-permute-start | bytes 49160 | tf_op jit(solution)/shard_map/ppermute | solution.py:22
  245.4 2.5 copy-start.6
  247.2 3.7 %copy-start.1 = (bf16[128,2048]{1,0:T(8,128)(2,1)S(1)}, bf16[128,2048]{1,0:T(8,128)(2,1)}, u32[]{:S(2)}) copy-start(bf16[128,2048]{1,0:T(8,128)(2,1)} %param.22) | copy-start | bytes 1572868
Sparse Core Ops, SparseCore 0:
  10.2 53.0 all-gather.8
  65.5 49.0 all-gather.6
  116.7 49.0 all-gather.4
  167.8 51.7 all-gather.10
